TPU v7x, 128 devices: a whole 4x4x4 slice. The times are simulated.
128 devices in a mesh: frame: 32 (over z, x_hi, y), head: 4 (over x_lo, core).
Axes of the slice: x: 4 (x_hi: 2, x_lo: 2; x = x_hi * 2 + x_lo), y: 4, z: 4, core: 2. Of those that a mesh axis runs over, the one named last changes fastest.
Arguments:
- queries: bfloat16 [24576, 5120], P('frame', 'head'), may hold values from -6.4 to 6.4
- keys: bfloat16 [24576, 5120], P('frame', 'head'), may hold values from -6.4 to 6.4
- values: bfloat16 [24576, 5120], P('frame', 'head'), may hold values from -6 to 6
- out_weight: bfloat16 [5120, 5120], P('head'), may hold values from -0.078125 to 0.078125
- sink_owner: int32 [32], replicated, may hold values from 0 to 31, each once
- frame_pos: int32 [32], P('frame'), may hold values from 0 to 93, as said below
Outputs:
- mixed: bfloat16 [24576, 5120], P('frame', 'head')
Inputs may be any that keep to these rules, and one draw needn't show every extreme that they name: `frame_pos`: strictly increasing, first entry 0, steps of 2 to 4. `sink_owner`: each number once.
All inputs are finite; a program needn't handle non-finite values.
Results may differ from a plain program's by a relative error of at most 0.01.
Values may be sent and summed in bfloat16 or wider, within the bound.
No kernel may reach another device: no remote copies, remote signals or barrier semaphores. Data moves between devices by JAX's collectives and lax.ppermute only.
A program may use at most 192 MiB of HBM per device.

v0:
```python
import jax
import jax.numpy as jnp
from jax import lax
from jax.sharding import PartitionSpec as P

HDIM = 128
GRID_W = 32


def shifted(array, axis, by):
    length = lax.axis_size(axis)
    pairs = [(i, i + by) for i in range(length) if 0 <= i + by < length]
    return lax.ppermute(array, axis, pairs)


def broadcast(value, axis, source):
    kept = jnp.where(lax.axis_index(axis) == source, value, 0).astype(value.dtype)
    return lax.psum(kept, axis)


def pair_angles(frame_value, count):
    half = HDIM // 2
    tdim = HDIM - 4 * (HDIM // 6)
    sdim = 2 * (HDIM // 6)
    tcount = tdim // 2
    scount = sdim // 2
    index = jnp.arange(half)
    findex = index.astype(jnp.float32)
    freq = jnp.where(
        index < tcount,
        jnp.power(10000.0, -2.0 * findex / tdim),
        jnp.where(
            index < tcount + scount,
            jnp.power(10000.0, -2.0 * (findex - tcount) / sdim),
            jnp.power(10000.0, -2.0 * (findex - tcount - scount) / sdim),
        ),
    )
    token = jnp.arange(count)
    row_pos = (token // GRID_W).astype(jnp.float32)[:, None]
    col_pos = (token % GRID_W).astype(jnp.float32)[:, None]
    frame_f = jnp.zeros((count, 1), jnp.float32) + frame_value.astype(jnp.float32)
    pos = jnp.where(
        index[None, :] < tcount,
        frame_f,
        jnp.where(index[None, :] < tcount + scount, row_pos, col_pos),
    )
    return pos * freq[None, :]


def rotate(block, angle):
    count = block.shape[0]
    heads_here = block.shape[1] // HDIM
    parts = block.astype(jnp.float32).reshape(count, heads_here, HDIM // 2, 2)
    cosine = jnp.cos(angle)[:, None, :]
    sine = jnp.sin(angle)[:, None, :]
    first = parts[..., 0] * cosine - parts[..., 1] * sine
    second = parts[..., 0] * sine + parts[..., 1] * cosine
    return (
        jnp.stack([first, second], axis=-1).reshape(count, heads_here * HDIM).astype(jnp.bfloat16)
    )


def attend_block(query, key_block, value_block):
    count = query.shape[0]
    heads_here = query.shape[1] // HDIM
    qh = query.reshape(count, heads_here, HDIM)
    kh = key_block.reshape(-1, heads_here, HDIM)
    vh = value_block.reshape(-1, heads_here, HDIM)
    scores = jnp.einsum("qhd,khd->hqk", qh, kh, preferred_element_type=jnp.float32) / jnp.sqrt(
        jnp.float32(HDIM)
    )
    peak = jnp.max(scores, axis=-1)
    weights = jnp.exp(scores - peak[..., None]).astype(jnp.bfloat16)
    total = jnp.sum(weights.astype(jnp.float32), axis=-1)
    partial_value = jnp.einsum("hqk,khd->hqd", weights, vh, preferred_element_type=jnp.float32)
    return (peak, total, partial_value)


def shards(queries, keys, values, out_weight, sink_owner, frame_pos):
    count = queries.shape[0]
    angle = pair_angles(frame_pos[0], count)
    rot_q = rotate(queries, angle)
    rot_k = rotate(keys, angle)
    place = lax.axis_index("frame")
    sink = sink_owner[0] % (lax.axis_size("frame") // 2)
    prev_k, prev_v = shifted((rot_k, values), "frame", 1)
    sink_k, sink_v = (broadcast(rot_k, "frame", sink), broadcast(values, "frame", sink))
    prev_used = (place >= 1) & (place - 1 != sink)
    sink_used = sink < place
    m_self, l_self, o_self = attend_block(rot_q, rot_k, values)
    m_prev, l_prev, o_prev = attend_block(rot_q, prev_k, prev_v)
    m_sink, l_sink, o_sink = attend_block(rot_q, sink_k, sink_v)
    top = jnp.maximum(m_self, jnp.where(prev_used, m_prev, m_self))
    top = jnp.maximum(top, jnp.where(sink_used, m_sink, m_self))
    c_self = jnp.exp(m_self - top)
    c_prev = jnp.where(prev_used, jnp.exp(m_prev - top), 0.0)
    c_sink = jnp.where(sink_used, jnp.exp(m_sink - top), 0.0)
    numer = o_self * c_self[..., None] + o_prev * c_prev[..., None] + o_sink * c_sink[..., None]
    denom = l_self * c_self + l_prev * c_prev + l_sink * c_sink
    attended = (
        jnp.transpose(numer / denom[..., None], (1, 0, 2)).reshape(count, -1).astype(jnp.bfloat16)
    )
    terms = jnp.dot(attended, out_weight, preferred_element_type=jnp.float32)
    mixed = lax.psum_scatter(terms.astype(jnp.bfloat16), "head", scatter_dimension=1, tiled=True)
    return mixed


def solution(mesh):
    in_specs = (
        P("frame", "head"),
        P("frame", "head"),
        P("frame", "head"),
        P("head", None),
        P(),
        P("frame"),
    )
    out_specs = P("frame", "head")
    return jax.shard_map(shards, mesh=mesh, in_specs=in_specs, out_specs=out_specs, check_vma=False)
```

profile of v0, /device:TPU:1, one launch (start us, length us, event | category | flops | bytes accessed | tf_op | source)
XLA Modules:
  0.0 553.0 jit_solution(17871531195031379992)
XLA Ops:
  6.5 5.4 collective-permute-start.1
  12.6 4.3 copy.19
  16.9 5.6 %reshape.273 = f32[768,10,64,2]{0,3,2,1:T(2,128)} reshape(f32[768,1280]{0,1:T(8,128)} %copy.19) | data formatting | bytes 7864320 | tf_op jit(solution)/shard_map/reshape | solution.py:53
  22.4 0.8 fusion.7
  23.2 7.0 %multiply_subtract_fusion = (bf16[768,10,64,1]{0,3,2,1:T(2,128)(2,1)S(1)}, bf16[768,10,64,1]{0,3,2,1:T(2,128)(2,1)S(1)}) fusion(f32[768,10,64,2]{0,3,2,1:T(2,128)} %reshape.273, f32[768,64]{0,1:T(8,128)S(1)} %get-tuple-element.16, f32[768,64]{0,1:T(8,128)S(1)} %get-tuple-element.15), kind=kLoop, calls=%fused_computation.20 | loop fusion | flops 3932160 | bytes 6291456 | tf_op jit(solution)/shard_map/sub | solution.py:56
  30.3 4.5 maximum_convert_fusion
  34.7 1.9 convert_element_type.83
  36.7 3.1 collective-permute-start
  39.9 2.7 copy.22
  42.6 1.6 broadcast_select_fusion.1
  44.2 1.4 broadcast_select_fusion
  45.6 4.0 copy.26
  50.3 5.2 convert_element_type.81
  55.5 4.3 copy.18
  59.8 5.6 %reshape.271 = f32[768,10,64,2]{0,3,2,1:T(2,128)} reshape(f32[768,1280]{0,1:T(8,128)} %copy.18) | data formatting | bytes 7864320 | tf_op jit(solution)/shard_map/reshape | solution.py:53
  65.4 7.0 %subtract_convert_fusion = (bf16[768,10,64,1]{0,3,2,1:T(2,128)(2,1)S(1)}, bf16[768,10,64,1]{0,3,2,1:T(2,128)(2,1)S(1)}) fusion(f32[768,10,64,2]{0,3,2,1:T(2,128)} %reshape.271, f32[768,64]{0,1:T(8,128)S(1)} %get-tuple-element.16, f32[768,64]{0,1:T(8,128)S(1)} %get-tuple-element.15), kind=kLoop, calls=%fused_computation.22 | loop fusion | flops 3932160 | bytes 6291456 | tf_op jit(solution)/shard_map/convert.2
  72.4 5.7 %pad_maximum_fusion = bf16[768,10,64,2]{0,3,2,1:T(2,128)(2,1)} fusion(bf16[768,10,64,1]{0,3,2,1:T(2,128)(2,1)S(1)} %get-tuple-element.12, bf16[768,10,64,1]{0,3,2,1:T(2,128)(2,1)S(1)} %get-tuple-element.11), kind=kLoop, calls=%fused_computation.18 | loop fusion | flops 3932160 | bytes 3932160 | tf_op jit(solution)/shard_map/stack | solution.py:59
  78.1 4.5 convert_element_type.79
  82.6 12.7 %multiply_reduce_fusion.2 = (f32[10,768]{1,0:T(8,128)S(1)}, f32[10,768,768]{1,2,0:T(8,128)}) fusion(bf16[768,10,128]{0,2,1:T(8,128)(2,1)S(1)} %convert_element_type.79, bf16[768,10,128]{0,2,1:T(8,128)(2,1)} %convert_element_type.81), kind=kOutput, calls=%fused_computation.8 | convolution fusion | flops 1521738240 | bytes 27555840 | tf_op jit(solution)/shard_map/qhd,khd->hqk/dot_general | solution.py:69
  95.3 10.6 %convert_reduce_fusion.2 = f32[10,768]{1,0:T(8,128)} fusion(f32[10,768]{1,0:T(8,128)S(1)} %get-tuple-element.19, f32[10,768,768]{1,2,0:T(8,128)} %get-tuple-element.20), kind=kLoop, calls=%fused_computation.2 | loop fusion | flops 29483520 | bytes 23654400 | tf_op jit(solution)/shard_map/reduce_sum | solution.py:74
  105.9 14.8 %fusion.4 = f32[10,768,128]{1,2,0:T(8,128)} fusion(bf16[768,10,128]{0,2,1:T(8,128)(2,1)} %bitcast.105, f32[10,768,768]{1,2,0:T(8,128)} %get-tuple-element.20, f32[10,768]{1,0:T(8,128)S(1)} %get-tuple-element.19), kind=kOutput, calls=%fused_computation.25 | convolution fusion | flops 1527644160 | bytes 29521920 | tf_op jit(solution)/shard_map/hqk,khd->hqd/dot_general | solution.py:75
  120.7 4.0 copy.28
  124.7 12.7 %multiply_reduce_fusion.1 = (f32[10,768]{1,0:T(8,128)S(1)}, f32[10,768,768]{1,2,0:T(8,128)}) fusion(bf16[768,10,128]{0,2,1:T(8,128)(2,1)S(1)} %convert_element_type.79, bf16[768,10,128]{0,2,1:T(8,128)(2,1)} %bitcast.5), kind=kOutput, calls=%fused_computation.7 | convolution fusion | flops 1521738240 | bytes 27555840 | tf_op jit(solution)/shard_map/qhd,khd->hqk/dot_general | solution.py:69
  137.4 10.9 %convert_reduce_fusion.1 = f32[10,768]{1,0:T(8,128)} fusion(f32[10,768]{1,0:T(8,128)S(1)} %get-tuple-element.21, f32[10,768,768]{1,2,0:T(8,128)} %get-tuple-element.22), kind=kLoop, calls=%fused_computation.1 | loop fusion | flops 29483520 | bytes 23654400 | tf_op jit(solution)/shard_map/reduce_sum | solution.py:74
  148.3 246.6 %all-reduce.3.cloned.1.call-done = (bf16[768,10,128]{0,2,1:T(8,128)(2,1)}, bf16[768,10,128]{2,0,1:T(8,128)(2,1)}) async-done(((bf16[768,10,128]{0,2,1:T(8,128)(2,1)}, bf16[768,10,128]{2,0,1:T(8,128)(2,1)}), (bf16[768,10,128]{0,2,1:T(8,128)(2,1)}, bf16[768,10,128]{2,0,1:T(8,128)(2,1)})) %all-reduce.3.cloned.1.call-update) | async-done | bytes 3932176 | tf_op jit(solution)/shard_map/psum | solution.py:18
  394.9 5.4 multiply_reduce_fusion
  400.3 7.2 %convert_reduce_fusion = f32[10,768]{1,0:T(8,128)} fusion(f32[10,768]{1,0:T(8,128)} %get-tuple-element.17, f32[10,768,768]{1,2,0:T(8,128)S(1)} %get-tuple-element.18), kind=kLoop, calls=%fused_computation | loop fusion | flops 29483520 | bytes 23654400 | tf_op jit(solution)/shard_map/reduce_sum | solution.py:74
  407.5 1.4 copy-done
  408.9 10.0 %fusion.5 = f32[10,768,128]{1,2,0:T(8,128)S(1)} fusion(bf16[768,10,128]{0,2,1:T(8,128)(2,1)S(1)} %copy-done.4, f32[10,768,768]{1,2,0:T(8,128)} %copy-done, f32[10,768]{1,0:T(8,128)} %get-tuple-element.17), kind=kOutput, calls=%fused_computation.26 | convolution fusion | flops 1527644160 | bytes 29521920 | tf_op jit(solution)/shard_map/hqk,khd->hqd/dot_general | solution.py:75
  419.0 11.8 %fusion.2 = bf16[768,10,128]{0,2,1:T(8,128)(2,1)} fusion(f32[10,768,128]{1,2,0:T(8,128)S(1)} %fusion.5, f32[10,768,128]{1,2,0:T(8,128)S(1)} %copy-done.3, bf16[768,10,128]{0,2,1:T(8,128)(2,1)} %bitcast.108, f32[768,10]{0,1:T(8,128)S(1)} %get-tuple-element.7, f32[768,10]{0,1:T(8,128)S(1)} %get-tuple-element.10, f32[768,10]{0,1:T(8,128)S(1)} %get-tuple-element.9, ...), kind=kOutput, calls=%fused_computation.14 | convolution fusion | flops 1534525440 | bytes 35543040 | tf_op jit(solution)/shard_map/hqk,khd->hqd/dot_general | solution.py:75
  430.8 17.9 %convolution_convert_fusion = bf16[768,5120]{1,0:T(8,128)(2,1)} fusion(bf16[768,1280]{0,1:T(8,128)(2,1)} %bitcast.112, bf16[1280,5120]{1,0:T(8,128)(2,1)} %param.9), kind=kOutput, calls=%fused_computation.9 | convolution fusion | flops 10070261760 | bytes 22937600 | tf_op jit(solution)/shard_map/dot_general | solution.py:103
  448.7 97.0 %reduce-scatter.2.cloned.1.call-done = bf16[768,1280]{1,0:T(8,128)(2,1)} async-done(((bf16[768,5120]{1,0:T(8,128)(2,1)}), bf16[768,1280]{1,0:T(8,128)(2,1)}) %reduce-scatter.2.cloned.1.call-update) | async-done | bytes 1966096 | tf_op jit(solution)/shard_map/reduce_scatter | solution.py:104
  (33 shorter events, 0.7 us)
Async XLA Ops:
  6.5 388.4 %all-reduce.3.cloned.1.call-start = ((), (), s32[]{:S(2)}) async-start(), calls=%async_computation.2 | async-start | bytes 7864320 | tf_op jit(solution)/shard_map/psum | solution.py:18
  6.5 114.2 %collective-permute-start.1 = (bf16[768,1280]{1,0:T(8,128)(2,1)}, bf16[768,1280]{1,0:T(8,128)(2,1)}, u32[]{:S(2)}, u32[]{:S(2)}) collective-permute-start(bf16[768,1280]{1,0:T(8,128)(2,1)} %param.8), channel_id=1, source_target_pairs={{0,4},{4,8},{8,12},{12,16},{16,20},{20,24},{24,28},{28,32},{32,36}... | collective-permute-start | bytes 5898248 | tf_op jit(solution)/shard_map/ppermute | solution.py:13
  30.3 9.5 %copy-start.11 = (s32[32]{0:T(128)S(1)}, s32[32]{0:T(128)}, u32[]{:S(2)}) copy-start(s32[32]{0:T(128)} %param.10) | copy-start | bytes 388
  34.7 5.2 copy-start.2
  36.7 88.1 %collective-permute-start = (bf16[768,1280]{0,1:T(8,128)(2,1)}, bf16[768,1280]{0,1:T(8,128)(2,1)}, u32[]{:S(2)}, u32[]{:S(2)}) collective-permute-start(bf16[768,1280]{0,1:T(8,128)(2,1)} %convert_element_type.83), channel_id=1, source_target_pairs={{0,4},{4,8},{8,12},{12,16},{16,20},{20,24},{24,28},{28,32},{32,36}... | collective-permute-start | bytes 5898248 | tf_op jit(solution)/shard_map/ppermute | solution.py:13
  42.6 17.1 %copy-start.1 = (bf16[768,1280]{0,1:T(8,128)(2,1)}, bf16[768,1280]{0,1:T(8,128)(2,1)S(1)}, u32[]{:S(2)}) copy-start(bf16[768,1280]{0,1:T(8,128)(2,1)S(1)} %copy.22) | copy-start | bytes 5898244
  49.7 496.1 %reduce-scatter.2.cloned.1.call-start = ((), (), s32[]{:S(2)}) async-start(), calls=%async_computation.1 | async-start | bytes 9830400 | tf_op jit(solution)/shard_map/reduce_scatter | solution.py:104
  137.4 10.9 %copy-start.6 = (f32[10,768]{1,0:T(8,128)}, f32[10,768]{1,0:T(8,128)S(1)}, u32[]{:S(2)}) copy-start(f32[10,768]{1,0:T(8,128)S(1)} %get-tuple-element.21) | copy-start | bytes 92164
  400.3 8.6 %copy-start = (f32[10,768,768]{1,2,0:T(8,128)}, f32[10,768,768]{1,2,0:T(8,128)S(1)}, u32[]{:S(2)}) copy-start(f32[10,768,768]{1,2,0:T(8,128)S(1)} %get-tuple-element.18) | copy-start | bytes 70778880
  400.3 8.6 %copy-start.4 = (bf16[768,10,128]{0,2,1:T(8,128)(2,1)S(1)}, bf16[768,10,128]{0,2,1:T(8,128)(2,1)}, u32[]{:S(2)}) copy-start(bf16[768,10,128]{0,2,1:T(8,128)(2,1)} %get-tuple-element.5) | copy-start | bytes 5898244
  408.9 10.0 %copy-start.5 = (f32[10,768]{1,0:T(8,128)S(1)}, f32[10,768]{1,0:T(8,128)}, u32[]{:S(2)}) copy-start(f32[10,768]{1,0:T(8,128)} %get-tuple-element.17) | copy-start | bytes 92164
  408.9 10.0 %copy-start.7 = (f32[10,768]{1,0:T(8,128)S(1)}, f32[10,768]{1,0:T(8,128)}, u32[]{:S(2)}) copy-start(f32[10,768]{1,0:T(8,128)} %copy-done.6) | copy-start | bytes 92164
  408.9 10.0 %copy-start.8 = (f32[10,768]{1,0:T(8,128)S(1)}, f32[10,768]{1,0:T(8,128)}, u32[]{:S(2)}) copy-start(f32[10,768]{1,0:T(8,128)} %convert_reduce_fusion.2) | copy-start | bytes 92164
  408.9 10.1 %copy-start.9 = (f32[10,768]{1,0:T(8,128)S(1)}, f32[10,768]{1,0:T(8,128)}, u32[]{:S(2)}) copy-start(f32[10,768]{1,0:T(8,128)} %convert_reduce_fusion.1) | copy-start | bytes 92164
  408.9 10.1 %copy-start.10 = (f32[10,768]{1,0:T(8,128)S(1)}, f32[10,768]{1,0:T(8,128)}, u32[]{:S(2)}) copy-start(f32[10,768]{1,0:T(8,128)} %convert_reduce_fusion) | copy-start | bytes 92164
  408.9 10.1 %copy-start.3 = (f32[10,768,128]{1,2,0:T(8,128)S(1)}, f32[10,768,128]{1,2,0:T(8,128)}, u32[]{:S(2)}) copy-start(f32[10,768,128]{1,2,0:T(8,128)} %fusion.4) | copy-start | bytes 11796484
Sparse Core Ops, SparseCore 0:
  49.8 345.0 all-reduce.2
  448.8 96.8 reduce-scatter.1
where the time goes:
time: 561 us; the launch traced here: 553 us
  waiting for transfers between devices  344 us (61%)
  matrix products  85.1 us (15%)
  other arithmetic  56.8 us (10%)
  local copies, waits for them, and re-layouts  43.5 us (8%)
  between operations  14.8 us (3%)
  starting transfers between devices  9.09 us (2%)
    psum x1, waiting for transfers between devices, broadcast(): return lax.psum(kept, axis)  247 us
    reduce_scatter x1, waiting for transfers between devices, shards(): lax.psum_scatter(terms.astype(jnp.bfloat16), 'head', scatter_dimension=1,...  97 us
    dot_general x3, matrix products, attend_block(): jnp.einsum('hqk,khd->hqd', weights, vh, preferred_element_type=jnp.float32)  36.5 us
    dot_general x3, matrix products, attend_block(): jnp.einsum('qhd,khd->hqk', qh, kh, preferred_element_type=jnp.float32)  30.8 us
    reduce_sum x3, other arithmetic, attend_block(): total = jnp.sum(weights.astype(jnp.float32), axis=-1)  28.7 us
    reshape x4, local copies, waits for them, and re-layouts, rotate(): parts = block.astype(jnp.float32).reshape(count, heads_here, HDIM // 2, 2)  19.7 us
    dot_general x1, matrix products, shards(): terms = jnp.dot(attended, out_weight, preferred_element_type=jnp.float32)  17.9 us
    convert_element_type x3, local copies, waits for them, and re-layouts, rotate(): jnp.stack([first, second], axis=-1).reshape(count, heads_here * HDIM)  11.6 us
  transfers between devices with their start and end apart: 4, of which 2 were waited for; matrix products, arithmetic and copies ran while one was open for 24% of the time, Pallas kernels for 0%

commit v1 on v0

--- a/solution.py
+++ b/solution.py
@@ -15,7 +15,7 @@
 
 def broadcast(value, axis, source):
     kept = jnp.where(lax.axis_index(axis) == source, value, 0).astype(value.dtype)
-    return lax.psum(kept, axis)
+    return jnp.sum(lax.all_gather(kept, axis), axis=0)
 
 
 def pair_angles(frame_value, count):

time: 561 us -> 1180 us (2.10)
  waiting for transfers between devices: 344 us -> 889 us
  other arithmetic: 56.8 us -> 107 us
    all_gather x0 -> x2, waiting for transfers between devices: none -> 807 us  [broadcast(): return jnp.sum(lax.all_gather(kept, axis), axis=0)]
    psum x1 -> x0, waiting for transfers between devices: 247 us -> none  [broadcast(): return lax.psum(kept, axis)]
    reduce_sum x0 -> x2, other arithmetic: none -> 45.5 us  [broadcast(): return jnp.sum(lax.all_gather(kept, axis), axis=0)]
    reduce_scatter x1, waiting for transfers between devices: 97 us -> 74.1 us  [shards(): lax.psum_scatter(terms.astype(jnp.bfloat16), 'head', scatter_dimension=1,...]
  transfers between devices with their start and end apart: 4 -> 5, of which waited for: 2 -> 4; matrix products, arithmetic and copies ran while one was open for 24% -> 14% of each run, Pallas kernels for 0% -> 0%
where the time goes in v1:
time: 1180 us; the launch traced here: 1170 us
  waiting for transfers between devices  889 us (75%)
  other arithmetic  107 us (9%)
  matrix products  93.8 us (8%)
  local copies, waits for them, and re-layouts  51.4 us (4%)
  between operations  16.5 us (1%)
    all_gather x2, waiting for transfers between devices, broadcast(): return jnp.sum(lax.all_gather(kept, axis), axis=0)  807 us
    reduce_scatter x1, waiting for transfers between devices, shards(): lax.psum_scatter(terms.astype(jnp.bfloat16), 'head', scatter_dimension=1,...  74.1 us
    reduce_sum x2, other arithmetic, broadcast(): return jnp.sum(lax.all_gather(kept, axis), axis=0)  45.5 us
    dot_general x3, matrix products, attend_block(): jnp.einsum('qhd,khd->hqk', qh, kh, preferred_element_type=jnp.float32)  40 us
    dot_general x3, matrix products, attend_block(): jnp.einsum('hqk,khd->hqd', weights, vh, preferred_element_type=jnp.float32)  35.9 us
    reduce_sum x3, other arithmetic, attend_block(): total = jnp.sum(weights.astype(jnp.float32), axis=-1)  31.7 us
  transfers between devices with their start and end apart: 5, of which 4 were waited for; matrix products, arithmetic and copies ran while one was open for 14% of the time, Pallas kernels for 0%

profile of v1, /device:TPU:1, one launch (start us, length us, event | category | flops | bytes accessed | tf_op | source)
XLA Modules:
  0.0 1167.9 jit_solution(10342810720730839764)
XLA Ops:
  13.6 5.6 reshape.290
  20.1 7.5 multiply_subtract_fusion
  27.5 6.3 broadcast_select_fusion
  33.8 5.3 select_n.175
  39.1 4.0 copy.67
  43.2 5.3 collective-permute-start.1
  50.2 5.3 collective-permute-start
  57.2 4.2 copy.59
  61.4 5.6 reshape.288
  67.0 7.1 subtract_convert_fusion
  74.1 5.7 pad_maximum_fusion
  79.8 4.5 convert_element_type.91
  84.3 12.6 %multiply_reduce_fusion.2 = (f32[10,768]{1,0:T(8,128)S(1)}, f32[10,768,768]{1,2,0:T(8,128)}) fusion(bf16[768,10,128]{0,2,1:T(8,128)(2,1)S(1)} %convert_element_type.91, bf16[768,10,128]{0,2,1:T(8,128)(2,1)} %convert_element_type.93), kind=kOutput, calls=%fused_computation.8 | convolution fusion | flops 1521738240 | bytes 27555840 | tf_op jit(solution)/shard_map/qhd,khd->hqk/dot_general | solution.py:69
  97.0 10.6 convert_reduce_fusion.2
  107.6 4.0 copy.63
  111.5 14.7 %fusion.4 = f32[10,768,128]{1,2,0:T(8,128)} fusion(bf16[768,10,128]{0,2,1:T(8,128)(2,1)} %bitcast.110, f32[10,768,768]{1,2,0:T(8,128)} %get-tuple-element.20, f32[10,768]{1,0:T(8,128)S(1)} %get-tuple-element.19), kind=kOutput, calls=%fused_computation.25 | convolution fusion | flops 1527644160 | bytes 29521920 | tf_op jit(solution)/shard_map/hqk,khd->hqd/dot_general | solution.py:75
  126.2 4.0 copy.71
  130.2 7.4 collective-permute-done
  137.6 14.8 %multiply_reduce_fusion.1 = (f32[10,768]{1,0:T(8,128)S(1)}, f32[10,768,768]{1,2,0:T(8,128)}) fusion(bf16[768,10,128]{0,2,1:T(8,128)(2,1)S(1)} %convert_element_type.91, bf16[768,10,128]{0,2,1:T(8,128)(2,1)} %bitcast.5), kind=kOutput, calls=%fused_computation.7 | convolution fusion | flops 1521738240 | bytes 27555840 | tf_op jit(solution)/shard_map/qhd,khd->hqk/dot_general | solution.py:69
  152.3 11.0 convert_reduce_fusion.1
  163.3 383.6 %all-gather.6.cloned.1.call-done = bf16[24576,1280]{1,0:T(8,128)(2,1)} async-done(((bf16[768,1280]{1,0:T(8,128)(2,1)}), bf16[24576,1280]{1,0:T(8,128)(2,1)}) %all-gather.6.cloned.1.call-update) | async-done | bytes 62914576 | tf_op jit(solution)/shard_map/all_gather | solution.py:18
  546.9 23.7 %reduce_sum.58 = bf16[768,1280]{1,0:T(8,128)(2,1)} reduce(bf16[32,768,1280]{2,1,0:T(8,128)(2,1)} %bitcast.108, bf16[]{:T(256)} %constant.89.clone.1), dimensions={0}, to_apply=%region_4.5 | reduce | flops 30474240 | bytes 64880640 | tf_op jit(solution)/shard_map/reduce_sum | solution.py:18
  570.6 4.0 copy.73
  574.7 423.7 %all-gather.4.cloned.1.call-done = bf16[32,768,1280]{2,1,0:T(8,128)(2,1)} async-done(((bf16[1,768,1280]{2,1,0:T(8,128)(2,1)}), bf16[32,768,1280]{2,1,0:T(8,128)(2,1)}) %all-gather.4.cloned.1.call-update) | async-done | bytes 62914576 | tf_op jit(solution)/shard_map/all_gather | solution.py:18
  998.3 21.7 %reduce_sum.57 = bf16[768,1280]{1,0:T(8,128)(2,1)} reduce(bf16[32,768,1280]{2,1,0:T(8,128)(2,1)} %all-gather.4.cloned.1.call-done, bf16[]{:T(256)} %constant.89.clone.1), dimensions={0}, to_apply=%region_2.3 | reduce | flops 30474240 | bytes 64880640 | tf_op jit(solution)/shard_map/reduce_sum | solution.py:18
  1020.1 4.1 copy.68
  1024.2 12.6 %multiply_reduce_fusion = (f32[10,768]{1,0:T(8,128)S(1)}, f32[10,768,768]{1,2,0:T(8,128)}) fusion(bf16[768,10,128]{0,2,1:T(8,128)(2,1)S(1)} %convert_element_type.91, bf16[768,10,128]{0,2,1:T(8,128)(2,1)} %bitcast.111), kind=kOutput, calls=%fused_computation.6 | convolution fusion | flops 1521738240 | bytes 27555840 | tf_op jit(solution)/shard_map/qhd,khd->hqk/dot_general | solution.py:69
  1036.8 10.1 convert_reduce_fusion
  1047.0 9.9 fusion.5
  1057.6 11.3 fusion.2
  1069.0 17.9 %convolution_convert_fusion = bf16[768,5120]{1,0:T(8,128)(2,1)} fusion(bf16[768,1280]{0,1:T(8,128)(2,1)} %bitcast.116, bf16[1280,5120]{1,0:T(8,128)(2,1)} %param.9), kind=kOutput, calls=%fused_computation.9 | convolution fusion | flops 10070261760 | bytes 22937600 | tf_op jit(solution)/shard_map/dot_general | solution.py:103
  1086.9 74.1 %reduce-scatter.2.cloned.1.call-done = bf16[768,1280]{1,0:T(8,128)(2,1)} async-done(((bf16[768,5120]{1,0:T(8,128)(2,1)}), bf16[768,1280]{1,0:T(8,128)(2,1)}) %reduce-scatter.2.cloned.1.call-update) | async-done | bytes 1966096 | tf_op jit(solution)/shard_map/reduce_scatter | solution.py:104
  (32 shorter events, 9.4 us)
Async XLA Ops:
  6.5 4.2 copy-start.2
  6.5 540.4 %all-gather.6.cloned.1.call-start = ((), (), s32[]{:S(2)}) async-start(), calls=%async_computation.3 | async-start | bytes 64880640 | tf_op jit(solution)/shard_map/all_gather | solution.py:18
  10.1 988.3 %all-gather.4.cloned.1.call-start = ((), (), s32[]{:S(2)}) async-start(), calls=%async_computation.1 | async-start | bytes 64880640 | tf_op jit(solution)/shard_map/all_gather | solution.py:18
  43.1 1117.9 %reduce-scatter.2.cloned.1.call-start = ((), (), s32[]{:S(2)}) async-start(), calls=%async_computation.2 | async-start | bytes 9830400 | tf_op jit(solution)/shard_map/reduce_scatter | solution.py:104
  43.2 83.1 %collective-permute-start.1 = (bf16[768,1280]{1,0:T(8,128)(2,1)}, bf16[768,1280]{1,0:T(8,128)(2,1)}, u32[]{:S(2)}, u32[]{:S(2)}) collective-permute-start(bf16[768,1280]{1,0:T(8,128)(2,1)} %param.8), channel_id=1, source_target_pairs={{0,4},{4,8},{8,12},{12,16},{16,20},{20,24},{24,28},{28,32},{32,36}... | collective-permute-start | bytes 5898248 | tf_op jit(solution)/shard_map/ppermute | solution.py:13
  50.2 87.4 %collective-permute-start = (bf16[768,1280]{0,1:T(8,128)(2,1)}, bf16[768,1280]{0,1:T(8,128)(2,1)}, u32[]{:S(2)}, u32[]{:S(2)}) collective-permute-start(bf16[768,1280]{0,1:T(8,128)(2,1)} %convert_element_type.95), channel_id=1, source_target_pairs={{0,4},{4,8},{8,12},{12,16},{16,20},{20,24},{24,28},{28,32},{32,36}... | collective-permute-start | bytes 5898248 | tf_op jit(solution)/shard_map/ppermute | solution.py:13
  152.3 11.0 copy-start.4
  1036.8 10.1 copy-start
  1046.9 10.0 copy-start.5
  1046.9 10.0 copy-start.6
  1046.9 10.0 copy-start.7
  1046.9 10.7 copy-start.1
  1046.9 10.7 copy-start.3
Sparse Core Ops, SparseCore 0:
  10.4 536.4 all-gather.5
  549.9 448.3 all-gather.3
  1087.0 73.9 reduce-scatter.1
